TPU v7x, 32 devices: a whole 2x2x4 slice. The times are simulated.
32 devices in a mesh: section: 4 (over y, x), mp: 2 (over core), dp: 4 (over z).
Axes of the slice: x: 2, y: 2, z: 4, core: 2. Of those that a mesh axis runs over, the one named last changes fastest.
Arguments:
- target_hidden: bfloat16 [4, 256, 8192], P('dp', None, 'section'), may hold values from -43 to 43, as said below
- embeds: bfloat16 [4, 256, 8192], P('dp', None, 'section'), may hold values from -50 to 50, as said below
- token_ids: int32 [4, 256], replicated, may hold values from 0 to 8191
- lengths: int32 [4], replicated, may hold values from 1 to 32, as said below
- offsets: int32 [4], replicated, may hold values from 0 to 224, as said below
- target_gain: float32 [8192], P('section'), may hold values from 0.5 to 1.5
- draft_gain: float32 [8192], P('section'), may hold values from 0.5 to 1.5
- head: bfloat16 [8192, 8192], P(('mp', 'dp'), 'section'), may hold values from -0.1875 to 0.1875
- fc_embed: bfloat16 [8192, 8192], P('section', ('mp', 'dp')), may hold values from -0.046875 to 0.046875
- fc_feature: bfloat16 [8192, 8192], P('section', ('mp', 'dp')), may hold values from -0.046875 to 0.046875
Outputs:
- loss: float32 [], replicated
- grad_embed: float32 [8192, 8192], P('section', ('mp', 'dp'))
- grad_feature: float32 [8192, 8192], P('section', ('mp', 'dp'))
Inputs may be any that keep to these rules, and one draw needn't show every extreme that they name: `lengths`: they sum to 64, and the longest response has exactly 32 rows. offsets + lengths <= 256 in every sequence; the sequence of the longest response starts at 224. `target_hidden`: real-valued features. `embeds`: real-valued embeddings.
All inputs are finite; a program needn't handle non-finite values.
Results may differ from a plain program's by a relative error of at most 0.0035.
The roundings to bfloat16 on the way count: a program that leaves them out, or rounds other values in their place, can miss the bound.
Values may be sent and summed in bfloat16 or wider, within the bound.
No kernel may reach another device: no remote copies, remote signals or barrier semaphores. Data moves between devices by JAX's collectives and lax.ppermute only.
A program may use at most 64 MiB of HBM per device.

v0:
```python
import jax
import jax.numpy as jnp
from jax import lax
from jax.sharding import PartitionSpec as P

D = 8192
R_OWN = 8
z_weight = 0.004
label_mix = 0.1
eps_norm = 1e-05


def contract_last(operand, weights):
    return lax.dot_general(
        operand, weights, (((1,), (1,)), ((), ())), preferred_element_type=jnp.float32
    )


def contract_first(operand, weights):
    return lax.dot_general(
        operand, weights, (((0,), (0,)), ((), ())), preferred_element_type=jnp.float32
    )


def sequence_of(packed, starts):
    return jnp.sum((starts[None, :] <= packed[:, None]).astype(jnp.int32), axis=1) - 1


def tile_sums(target_logit, draft_logit, labels, column_zero):
    is_label = (
        labels[:, None] - column_zero == jnp.arange(target_logit.shape[1], dtype=jnp.int32)[None, :]
    )
    target_exp = jnp.exp(target_logit)
    return (
        jnp.sum(target_exp, axis=1),
        jnp.sum(target_exp * draft_logit, axis=1),
        jnp.sum(jnp.exp(draft_logit), axis=1),
        jnp.sum(jnp.where(is_label, draft_logit, 0.0), axis=1),
    )


def tile_grad(target_logit, draft_logit, labels, column_zero, totals):
    target_total, cross_total, draft_total, label_logit = totals
    draft_lse = jnp.log(draft_total)
    target_lse = jnp.log(target_total)
    is_label = (
        labels[:, None] - column_zero == jnp.arange(target_logit.shape[1], dtype=jnp.int32)[None, :]
    )
    logit_grad = (
        (1.0 + 2.0 * z_weight * draft_lse)[:, None] * jnp.exp(draft_logit - draft_lse[:, None])
        - (1.0 - label_mix) * jnp.exp(target_logit - target_lse[:, None])
        - label_mix * is_label.astype(jnp.float32)
    )
    return logit_grad.astype(jnp.bfloat16)


def mean_loss(totals):
    target_total, cross_total, draft_total, label_logit = totals
    draft_lse = jnp.log(draft_total)
    row_loss = (
        draft_lse
        - (1.0 - label_mix) * cross_total / target_total
        - label_mix * label_logit
        + z_weight * draft_lse * draft_lse
    )
    return jnp.mean(row_loss)


def on_device(
    target_hidden,
    embeds,
    token_ids,
    lengths,
    offsets,
    target_gain,
    draft_gain,
    head,
    fc_embed,
    fc_feature,
):
    count_dp = lax.axis_size("dp")
    count_mp = lax.axis_size("mp")
    groups = count_mp * count_dp
    my_dp = lax.axis_index("dp")
    my_mp = lax.axis_index("mp")
    owner_index = my_mp * count_dp + my_dp
    section_index = lax.axis_index("section")
    slice_width = target_hidden.shape[2]
    seq_len = target_hidden.shape[1]
    vocab_tile = head.shape[0]
    slot_count = 2 * R_OWN // count_dp
    total_rows = R_OWN * groups
    starts = jnp.cumsum(lengths) - lengths
    first_row = starts[my_dp]
    my_count = lengths[my_dp]
    my_offset = offsets[my_dp]
    residue = my_mp * count_dp + jnp.arange(count_dp, dtype=jnp.int32)
    first_slot = (first_row - residue + groups - 1) // groups
    packed = (
        groups * (first_slot[:, None] + jnp.arange(slot_count, dtype=jnp.int32)[None, :])
        + residue[:, None]
    )
    is_live = (packed < first_row + my_count).reshape(-1, 1)
    flat_position = jnp.clip(my_offset + packed - first_row, 0, seq_len - 1).reshape(-1)
    taken_embed = jnp.take(embeds[0], flat_position, axis=0)
    taken_feature = jnp.take(target_hidden[0], flat_position, axis=0)
    send_embed = jnp.where(is_live, taken_embed, jnp.zeros_like(taken_embed)).reshape(
        count_dp, slot_count, slice_width
    )
    send_feature = jnp.where(is_live, taken_feature, jnp.zeros_like(taken_feature)).reshape(
        count_dp, slot_count, slice_width
    )
    got_embed, got_feature = (
        lax.all_to_all(send_embed, "dp", split_axis=0, concat_axis=0, tiled=True),
        lax.all_to_all(send_feature, "dp", split_axis=0, concat_axis=0, tiled=True),
    )
    slot_index = jnp.arange(R_OWN, dtype=jnp.int32)
    wanted = groups * slot_index + owner_index
    source = sequence_of(wanted, starts)
    source_first = (starts[source] - owner_index + groups - 1) // groups
    pick_index = source * slot_count + slot_index - source_first
    own_embed = jnp.take(got_embed.reshape(count_dp * slot_count, slice_width), pick_index, axis=0)
    own_feature = jnp.take(
        got_feature.reshape(count_dp * slot_count, slice_width), pick_index, axis=0
    )
    embed_all, feature_all = (
        lax.all_gather(own_embed, ("mp", "dp"), axis=0, tiled=True),
        lax.all_gather(own_feature, ("mp", "dp"), axis=0, tiled=True),
    )
    row_id = jnp.arange(total_rows, dtype=jnp.int32)
    packed_all = groups * (row_id % R_OWN) + row_id // R_OWN
    seq_all = sequence_of(packed_all, starts)
    position_all = offsets[seq_all] + packed_all - starts[seq_all]
    labels = token_ids.reshape(-1)[seq_all * seq_len + position_all]
    target_square = lax.psum(
        jnp.sum(jnp.square(feature_all.astype(jnp.float32)), axis=1), "section"
    )
    target_scale = lax.rsqrt(target_square / D + eps_norm)
    target_norm = (feature_all.astype(jnp.float32) * target_scale[:, None] * target_gain).astype(
        jnp.bfloat16
    )
    partial_value = jnp.dot(embed_all, fc_embed, preferred_element_type=jnp.float32) + jnp.dot(
        feature_all, fc_feature, preferred_element_type=jnp.float32
    )
    summed = lax.psum(partial_value, "section")
    spread = lax.all_to_all(summed, ("mp", "dp"), split_axis=0, concat_axis=1, tiled=True)
    hidden = lax.dynamic_slice_in_dim(spread, section_index * slice_width, slice_width, 1)
    draft_square = lax.psum(jnp.sum(hidden * hidden, axis=1), "section")
    draft_scale = lax.rsqrt(draft_square / D + eps_norm)
    draft_norm = (hidden * draft_scale[:, None] * draft_gain).astype(jnp.bfloat16)
    target_part = contract_last(target_norm, head)
    draft_part = contract_last(lax.all_gather(draft_norm, ("mp", "dp"), axis=0, tiled=True), head)
    target_logit, draft_logit = lax.psum((target_part, draft_part), "section")
    column_zero = owner_index * vocab_tile
    totals = lax.psum(tile_sums(target_logit, draft_logit, labels, column_zero), ("mp", "dp"))
    grad_tile = tile_grad(target_logit, draft_logit, labels, column_zero, totals)
    loss = mean_loss(totals)
    draft_grad = lax.psum_scatter(
        jnp.dot(grad_tile, head, preferred_element_type=jnp.float32),
        ("mp", "dp"),
        scatter_dimension=0,
        tiled=True,
    )
    upstream = draft_grad * draft_gain
    inner_sum = lax.psum(jnp.sum(hidden * upstream, axis=1), "section")
    hidden_grad = (
        draft_scale[:, None] * upstream - hidden * (draft_scale**3 * inner_sum / D)[:, None]
    ).astype(jnp.bfloat16)
    full_grad = lax.all_gather(hidden_grad, "section", axis=1, tiled=True)
    block_grad = lax.all_to_all(full_grad, ("mp", "dp"), split_axis=1, concat_axis=0, tiled=True)
    grad_embed = contract_first(embed_all, block_grad)
    grad_feature = contract_first(feature_all, block_grad)
    return (loss, grad_embed, grad_feature)


def solution(mesh):
    return jax.shard_map(
        on_device,
        mesh=mesh,
        in_specs=(
            P("dp", None, "section"),
            P("dp", None, "section"),
            P(),
            P(),
            P(),
            P("section"),
            P("section"),
            P(("mp", "dp"), "section"),
            P("section", ("mp", "dp")),
            P("section", ("mp", "dp")),
        ),
        out_specs=(P(), P("section", ("mp", "dp")), P("section", ("mp", "dp"))),
        check_vma=False,
    )
```

profile of v0, /device:TPU:0, one launch (start us, length us, event | category | flops | bytes accessed | tf_op | source)
XLA Modules:
  0.0 335.6 jit_solution(14348024160950690089)
XLA Ops:
  18.6 6.3 %all-to-all-start.1 = ((bf16[4,4,2048]{2,1,0:T(4,128)(2,1)}), bf16[4,4,2048]{2,1,0:T(4,128)(2,1)S(1)}, u32[]{:S(2)}, u32[]{:S(2)}) async-start(bf16[4,4,2048]{2,1,0:T(4,128)(2,1)} %reshape.273), calls=%async_computation.1 | async-start | bytes 131072 | tf_op jit(solution)/shard_map/all_to_all | solution.py:115
  26.4 4.3 %all-to-all-done.1 = bf16[4,4,2048]{2,1,0:T(4,128)(2,1)S(1)} async-done(((bf16[4,4,2048]{2,1,0:T(4,128)(2,1)}), bf16[4,4,2048]{2,1,0:T(4,128)(2,1)S(1)}, u32[]{:S(2)}, u32[]{:S(2)}) %all-to-all-start.1) | async-done | bytes 65568 | tf_op jit(solution)/shard_map/all_to_all | solution.py:115
  30.7 3.3 all-to-all-start
  34.7 5.0 %all-to-all-done = bf16[4,4,2048]{2,1,0:T(4,128)(2,1)S(1)} async-done(((bf16[4,4,2048]{2,1,0:T(4,128)(2,1)}), bf16[4,4,2048]{2,1,0:T(4,128)(2,1)S(1)}, u32[]{:S(2)}, u32[]{:S(2)}) %all-to-all-start) | async-done | bytes 65568 | tf_op jit(solution)/shard_map/all_to_all | solution.py:114
  40.4 24.4 %all_gather.13 = bf16[64,2048]{1,0:T(8,128)(2,1)S(1)} all-gather(bf16[8,2048]{1,0:T(8,128)(2,1)S(1)} %get-tuple-element.35), channel_id=1, replica_groups=mesh['section'=4,'mp'=2,'dp'=4] {'mp','dp'}, dimensions={0}, use_global_device_ids=true | all-gather | bytes 294912 | tf_op jit(solution)/shard_map/all_gather | solution.py:128
  64.9 24.3 %all_gather.12 = bf16[64,2048]{1,0:T(8,128)(2,1)S(1)} all-gather(bf16[8,2048]{1,0:T(8,128)(2,1)S(1)} %get-tuple-element.36), channel_id=1, replica_groups=mesh['section'=4,'mp'=2,'dp'=4] {'mp','dp'}, dimensions={0}, use_global_device_ids=true | all-gather | bytes 294912 | tf_op jit(solution)/shard_map/all_gather | solution.py:127
  89.1 3.0 fusion.39
  93.8 43.6 %all-reduce.6.cloned.1.call-done = f32[8,8,1024]{2,1,0:T(8,128)} async-done(((f32[8,8,1024]{2,1,0:T(8,128)}), f32[8,8,1024]{2,1,0:T(8,128)}) %all-reduce.6.cloned.1.call-update) | async-done | bytes 262160 | tf_op jit(solution)/shard_map/psum | solution.py:145
  137.4 4.6 %all-to-all-start.2 = ((f32[8,8,1024]{2,1,0:T(8,128)}), f32[8,8,1024]{2,1,0:T(8,128)S(1)}, u32[]{:S(2)}, u32[]{:S(2)}) async-start(f32[8,8,1024]{2,1,0:T(8,128)} %all-reduce.6.cloned.1.call-done), calls=%async_computation.2 | async-start | bytes 524288 | tf_op jit(solution)/shard_map/all_to_all | solution.py:146
  142.3 9.1 %all-to-all-done.2 = f32[8,8,1024]{2,1,0:T(8,128)S(1)} async-done(((f32[8,8,1024]{2,1,0:T(8,128)}), f32[8,8,1024]{2,1,0:T(8,128)S(1)}, u32[]{:S(2)}, u32[]{:S(2)}) %all-to-all-start.2) | async-done | bytes 262176 | tf_op jit(solution)/shard_map/all_to_all | solution.py:146
  151.5 8.9 %all-reduce.1 = (f32[8]{0:T(128)S(1)}, f32[64]{0:T(128)S(1)}) all-reduce(f32[8]{0:T(128)S(1)} %multiply_reduce_fusion.2, f32[64]{0:T(128)S(1)} %fusion.1), channel_id=1, replica_groups=mesh['section'=4,'mp'=2,'dp'=4] {'section'}, use_global_device_ids=true, to_apply=%region_4.7 | all-reduce | flops 72 | bytes 576 | tf_op jit(solution)/shard_map/psum | solution.py:148
  160.6 24.4 %all_gather.14 = bf16[64,2048]{1,0:T(8,128)(2,1)S(1)} all-gather(bf16[8,2048]{1,0:T(8,128)(2,1)S(1)} %multiply_convert_fusion), channel_id=1, replica_groups=mesh['section'=4,'mp'=2,'dp'=4] {'mp','dp'}, dimensions={0}, use_global_device_ids=true | all-gather | bytes 294912 | tf_op jit(solution)/shard_map/all_gather | solution.py:152
  185.0 4.3 %fusion.40 = f32[64,1024]{1,0:T(8,128)} fusion(bf16[64,2048]{1,0:T(8,128)(2,1)S(1)} %all_gather.14, bf16[1024,2048]{1,0:T(8,128)(2,1)} %param.21), kind=kOutput, calls=%fused_computation.111 | convolution fusion | flops 268435456 | bytes 4718592 | tf_op jit(solution)/shard_map/dot_general | solution.py:14
  191.5 5.1 %fusion.31 = s32[64]{0:T(128)S(1)} fusion(s32[64]{0:T(128)S(1)} %convert_reduce_fusion, s32[]{:T(128)} %bitcast.19, s32[]{:T(128)} %bitcast.15, s32[]{:T(128)} %bitcast.20, s32[]{:T(128)} %bitcast.16, s32[]{:T(128)} %bitcast.22, s32[]{:T(128)} %bitcast.21, s32[]{:T(128)} %bitcast.18, s32[]{:T(128)} %bitcast.17), kind=kLoop, calls=%fused_computation.94 | loop fusion | flops 2176 | bytes 544 | tf_op jit(solution)/shard_map/select_n | solution.py:134
  197.3 37.7 %all-reduce.8.cloned.1.call-done = (f32[64,1024]{1,0:T(8,128)}, f32[64,1024]{1,0:T(8,128)}) async-done(((f32[64,1024]{1,0:T(8,128)}, f32[64,1024]{1,0:T(8,128)}), (f32[64,1024]{1,0:T(8,128)}, f32[64,1024]{1,0:T(8,128)})) %all-reduce.8.cloned.1.call-update) | async-done | bytes 524304 | tf_op jit(solution)/shard_map/psum | solution.py:153
  236.3 15.9 %all-reduce = (f32[64]{0:T(128)S(1)}, f32[64]{0:T(128)S(1)}, f32[64]{0:T(128)S(1)}, f32[64]{0:T(128)S(1)}) all-reduce(f32[64]{0:T(128)S(1)} %get-tuple-element.6, f32[64]{0:T(128)S(1)} %get-tuple-element.8, f32[64]{0:T(128)S(1)} %get-tuple-element.7, f32[64]{0:T(128)S(1)} %get-tuple-element.5), channel_id=1, replica_groups=mesh['section'=4,'mp'=2,'dp'=4] {'mp','dp'}, use_global_device_ids=true, to_apply=%region_17.20 | all-reduce | flops 256 | bytes 2048 | tf_op jit(solution)/shard_map/psum | solution.py:155
  252.8 4.1 %fusion.8 = f32[64,2048]{1,0:T(8,128)} fusion(bf16[1024,2048]{1,0:T(8,128)(2,1)} %param.21, f32[64,1024]{1,0:T(8,128)} %get-tuple-element.16, f32[64,1024]{1,0:T(8,128)} %get-tuple-element.15, f32[64]{0:T(128)S(1)} %get-tuple-element.23, f32[64]{0:T(128)S(1)} %get-tuple-element.24, f32[64]{0:T(128)S(1)} %get-tuple-element.21, s32[64]{0:T(128)S(1)} %broadcast_subtract_fusion), kind=kOutput, calls=%fused_computation.22 | convolution fusion | flops 269025280 | bytes 5243904 | tf_op jit(solution)/shard_map/dot_general | solution.py:159
  257.0 31.1 %reduce-scatter.2.cloned.1.call-done = f32[8,2048]{1,0:T(8,128)} async-done(((f32[64,2048]{1,0:T(8,128)}), f32[8,2048]{1,0:T(8,128)}) %reduce-scatter.2.cloned.1.call-update) | async-done | bytes 65552 | tf_op jit(solution)/shard_map/reduce_scatter | solution.py:158
  289.1 10.0 %psum.79 = f32[8]{0:T(128)S(1)} all-reduce(f32[8]{0:T(128)S(1)} %multiply_reduce_fusion.1), channel_id=1, replica_groups=mesh['section'=4,'mp'=2,'dp'=4] {'section'}, use_global_device_ids=true, to_apply=%region_21.24 | all-reduce | flops 8 | bytes 64 | tf_op jit(solution)/shard_map/psum | solution.py:165
  300.0 8.3 %all_gather.15 = bf16[8,8192]{1,0:T(8,128)(2,1)} all-gather(bf16[8,2048]{1,0:T(8,128)(2,1)S(1)} %subtract_convert_fusion.2), channel_id=1, replica_groups=mesh['section'=4,'mp'=2,'dp'=4] {'section'}, dimensions={1}, use_global_device_ids=true | all-gather | bytes 163840 | tf_op jit(solution)/shard_map/all_gather | solution.py:169
  308.3 3.4 %all-to-all-start.3 = ((bf16[8,8,1024]{2,0,1:T(8,128)(2,1)}), bf16[8,8,1024]{2,0,1:T(8,128)(2,1)S(1)}, u32[]{:S(2)}, u32[]{:S(2)}) async-start(bf16[8,8,1024]{2,0,1:T(8,128)(2,1)} %bitcast.24), calls=%async_computation.4 | async-start | bytes 262144 | tf_op jit(solution)/shard_map/all_to_all | solution.py:170
  312.3 6.2 %all-to-all-done.3 = bf16[8,8,1024]{2,0,1:T(8,128)(2,1)S(1)} async-done(((bf16[8,8,1024]{2,0,1:T(8,128)(2,1)}), bf16[8,8,1024]{2,0,1:T(8,128)(2,1)S(1)}, u32[]{:S(2)}, u32[]{:S(2)}) %all-to-all-start.3) | async-done | bytes 131104 | tf_op jit(solution)/shard_map/all_to_all | solution.py:170
  318.5 4.7 %fusion.9 = f32[2048,1024]{1,0:T(8,128)} fusion(bf16[64,2048]{1,0:T(8,128)(2,1)S(1)} %all_gather.13, bf16[8,8,1024]{2,0,1:T(8,128)(2,1)S(1)} %all-to-all-done.3), kind=kOutput, calls=%fused_computation.23 | convolution fusion | flops 268435456 | bytes 8781824 | tf_op jit(solution)/shard_map/dot_general | solution.py:20
  323.2 4.7 %fusion.11 = f32[2048,1024]{1,0:T(8,128)} fusion(bf16[64,2048]{1,0:T(8,128)(2,1)S(1)} %all_gather.12, bf16[8,8,1024]{2,0,1:T(8,128)(2,1)S(1)} %all-to-all-done.3), kind=kOutput, calls=%fused_computation.25 | convolution fusion | flops 268435456 | bytes 8781824 | tf_op jit(solution)/shard_map/dot_general | solution.py:20
  (66 shorter events, 21.7 us)
Async XLA Ops:
  7.2 8.1 %copy-start = (bf16[1,256,2048]{2,1,0:T(8,128)(2,1)S(1)}, bf16[1,256,2048]{2,1,0:T(8,128)(2,1)}, u32[]{:S(2)}) copy-start(bf16[1,256,2048]{2,1,0:T(8,128)(2,1)} %param.14) | copy-start | bytes 3145732
  18.6 12.1 %all-to-all-start.1 = ((bf16[4,4,2048]{2,1,0:T(4,128)(2,1)}), bf16[4,4,2048]{2,1,0:T(4,128)(2,1)S(1)}, u32[]{:S(2)}, u32[]{:S(2)}) async-start(bf16[4,4,2048]{2,1,0:T(4,128)(2,1)} %reshape.273), calls=%async_computation.1 | async-start | bytes 131072 | tf_op jit(solution)/shard_map/all_to_all | solution.py:115
  30.7 9.0 %all-to-all-start = ((bf16[4,4,2048]{2,1,0:T(4,128)(2,1)}), bf16[4,4,2048]{2,1,0:T(4,128)(2,1)S(1)}, u32[]{:S(2)}, u32[]{:S(2)}) async-start(bf16[4,4,2048]{2,1,0:T(4,128)(2,1)} %reshape.271), calls=%async_computation | async-start | bytes 131072 | tf_op jit(solution)/shard_map/all_to_all | solution.py:114
  34.0 103.4 %all-reduce.6.cloned.1.call-start = ((), (), s32[]{:S(2)}) async-start(), calls=%async_computation.5 | async-start | bytes 524288 | tf_op jit(solution)/shard_map/psum | solution.py:145
  40.3 51.8 %copy-start.2 = (bf16[2048,1024]{1,0:T(8,128)(2,1)S(1)}, bf16[2048,1024]{1,0:T(8,128)(2,1)}, u32[]{:S(2)}) copy-start(bf16[2048,1024]{1,0:T(8,128)(2,1)} %param.23) | copy-start | bytes 12582916
  92.2 59.3 %copy-start.5 = (s32[4,256]{1,0:T(4,128)S(1)}, s32[4,256]{1,0:T(4,128)}, u32[]{:S(2)}) copy-start(s32[4,256]{1,0:T(4,128)} %param.16) | copy-start | bytes 12292
  92.2 68.3 %copy-start.3 = (f32[2048]{0:T(1024)S(1)}, f32[2048]{0:T(1024)}, u32[]{:S(2)}) copy-start(f32[2048]{0:T(1024)} %param.20) | copy-start | bytes 24580
  93.7 95.5 %copy-start.4 = (f32[2048]{0:T(1024)S(1)}, f32[2048]{0:T(1024)}, u32[]{:S(2)}) copy-start(f32[2048]{0:T(1024)} %param.19) | copy-start | bytes 24580
  137.4 14.0 %all-to-all-start.2 = ((f32[8,8,1024]{2,1,0:T(8,128)}), f32[8,8,1024]{2,1,0:T(8,128)S(1)}, u32[]{:S(2)}, u32[]{:S(2)}) async-start(f32[8,8,1024]{2,1,0:T(8,128)} %all-reduce.6.cloned.1.call-done), calls=%async_computation.2 | async-start | bytes 524288 | tf_op jit(solution)/shard_map/all_to_all | solution.py:146
  142.0 93.0 %all-reduce.8.cloned.1.call-start = ((), (), s32[]{:S(2)}) async-start(), calls=%async_computation.7 | async-start | bytes 1048576 | tf_op jit(solution)/shard_map/psum | solution.py:153
  160.5 28.8 %copy-start.1 = (bf16[1024,2048]{1,0:T(8,128)(2,1)S(1)}, bf16[1024,2048]{1,0:T(8,128)(2,1)}, u32[]{:S(2)}) copy-start(bf16[1024,2048]{1,0:T(8,128)(2,1)} %param.21) | copy-start | bytes 12582916
  191.4 96.7 %reduce-scatter.2.cloned.1.call-start = ((), (), s32[]{:S(2)}) async-start(), calls=%async_computation.6 | async-start | bytes 589824 | tf_op jit(solution)/shard_map/reduce_scatter | solution.py:158
  308.3 10.2 %all-to-all-start.3 = ((bf16[8,8,1024]{2,0,1:T(8,128)(2,1)}), bf16[8,8,1024]{2,0,1:T(8,128)(2,1)S(1)}, u32[]{:S(2)}, u32[]{:S(2)}) async-start(bf16[8,8,1024]{2,0,1:T(8,128)(2,1)} %bitcast.24), calls=%async_computation.4 | async-start | bytes 262144 | tf_op jit(solution)/shard_map/all_to_all | solution.py:170
Sparse Core Ops, SparseCore 0:
  93.9 43.4 all-reduce.5
  191.6 43.4 all-reduce.7
  257.1 30.9 reduce-scatter.1
where the time goes:
time: 337 us; the launch traced here: 336 us
  waiting for transfers between devices  137 us (41%)
  blocking collectives  116 us (34%)
  matrix products  24.4 us (7%)
  starting transfers between devices  17.7 us (5%)
  between operations  17.1 us (5%)
  other arithmetic  13.2 us (4%)
  local copies, waits for them, and re-layouts  9.64 us (3%)
    psum x1, waiting for transfers between devices, on_device(): summed = lax.psum(partial_value, 'section')  43.6 us
    psum x1, waiting for transfers between devices, on_device(): target_logit, draft_logit = lax.psum((target_part, draft_part), 'section')  37.7 us
    reduce_scatter x1, waiting for transfers between devices, on_device(): lax.psum_scatter(jnp.dot(grad_tile, head, preferred_element_type=jnp.floa...  31.1 us
    all_gather x1, blocking collectives, on_device(): lax.all_gather(own_feature, ('mp', 'dp'), axis=0, tiled=True)  24.4 us
    all_gather x1, blocking collectives, on_device(): lax.all_gather(draft_norm, ('mp', 'dp'), axis=0, tiled=True)  24.4 us
    all_gather x1, blocking collectives, on_device(): lax.all_gather(own_embed, ('mp', 'dp'), axis=0, tiled=True)  24.3 us
    psum x1, blocking collectives, on_device(): lax.psum(tile_sums(target_logit, draft_logit, labels, column_zero), ('mp'...  15.9 us
    psum x1, blocking collectives, on_device(): inner_sum = lax.psum(jnp.sum(hidden * upstream, axis=1), 'section')  9.95 us
  transfers between devices with their start and end apart: 7, of which 7 were waited for; matrix products, arithmetic and copies ran while one was open for 2% of the time, Pallas kernels for 0%

commit v1 on v0

--- a/solution.py
+++ b/solution.py
@@ -8,6 +8,17 @@
 z_weight = 0.004
 label_mix = 0.1
 eps_norm = 1e-05
+
+
+def cut_along(x, dim, size):
+    before, after = (x.shape[:dim], x.shape[dim + 1 :])
+    return jnp.moveaxis(x.reshape(*before, size, -1, *after), dim, 0)
+
+
+def laid_out(pieces, dim):
+    pieces = jnp.moveaxis(pieces, 0, dim)
+    dims = pieces.shape
+    return pieces.reshape(*dims[:dim], dims[dim] * dims[dim + 1], *dims[dim + 2 :])
 
 
 def contract_last(operand, weights):
@@ -143,7 +154,14 @@
         feature_all, fc_feature, preferred_element_type=jnp.float32
     )
     summed = lax.psum(partial_value, "section")
-    spread = lax.all_to_all(summed, ("mp", "dp"), split_axis=0, concat_axis=1, tiled=True)
+    peers, here = (lax.axis_size(("mp", "dp")), lax.axis_index(("mp", "dp")))
+    blocks = cut_along(summed, 0, peers)
+    finished = [blocks[here]]
+    for hop in range(1, peers):
+        sent = blocks[here ^ hop]
+        finished.append(lax.ppermute(sent, ("mp", "dp"), [(i, i ^ hop) for i in range(peers)]))
+    blocks = jnp.stack(finished)[here ^ jnp.arange(peers)]
+    spread = laid_out(blocks, 1)
     hidden = lax.dynamic_slice_in_dim(spread, section_index * slice_width, slice_width, 1)
     draft_square = lax.psum(jnp.sum(hidden * hidden, axis=1), "section")
     draft_scale = lax.rsqrt(draft_square / D + eps_norm)

time: 337 us -> 342 us (1.015)
  starting transfers between devices: 17.7 us -> 23.1 us
    ppermute x0 -> x7, starting transfers between devices: none -> 9.99 us  [on_device(): lax.ppermute(sent, ('mp', 'dp'), [(i, i ^ hop) for i in range(peers)])]
    all_to_all x1 -> x0, waiting for transfers between devices: 9.06 us -> none  [on_device(): lax.all_to_all(summed, ('mp', 'dp'), split_axis=0, concat_axis=1, tiled=T...]
    ppermute x0 -> x7, waiting for transfers between devices: none -> 6.46 us  [on_device(): lax.ppermute(sent, ('mp', 'dp'), [(i, i ^ hop) for i in range(peers)])]
    all_to_all x1 -> x0, starting transfers between devices: 4.61 us -> none  [on_device(): lax.all_to_all(summed, ('mp', 'dp'), split_axis=0, concat_axis=1, tiled=T...]
  transfers between devices with their start and end apart: 7 -> 13, of which waited for: 7 -> 8; matrix products, arithmetic and copies ran while one was open for 2% -> 2% of each run, Pallas kernels for 0% -> 0%
where the time goes in v1:
time: 342 us; the launch traced here: 341 us
  waiting for transfers between devices  135 us (39%)
  blocking collectives  116 us (34%)
  matrix products  24.4 us (7%)
  starting transfers between devices  23.1 us (7%)
  between operations  17.2 us (5%)
  other arithmetic  13.3 us (4%)
  local copies, waits for them, and re-layouts  11.1 us (3%)
    psum x1, waiting for transfers between devices, on_device(): summed = lax.psum(partial_value, 'section')  43.4 us
    psum x1, waiting for transfers between devices, on_device(): target_logit, draft_logit = lax.psum((target_part, draft_part), 'section')  38.9 us
    reduce_scatter x1, waiting for transfers between devices, on_device(): lax.psum_scatter(jnp.dot(grad_tile, head, preferred_element_type=jnp.floa...  31.1 us
    all_gather x1, blocking collectives, on_device(): lax.all_gather(draft_norm, ('mp', 'dp'), axis=0, tiled=True)  24.6 us
    all_gather x1, blocking collectives, on_device(): lax.all_gather(own_feature, ('mp', 'dp'), axis=0, tiled=True)  24.4 us
    all_gather x1, blocking collectives, on_device(): lax.all_gather(own_embed, ('mp', 'dp'), axis=0, tiled=True)  24.3 us
    psum x1, blocking collectives, on_device(): lax.psum(tile_sums(target_logit, draft_logit, labels, column_zero), ('mp'...  15.9 us
    ppermute x7, starting transfers between devices, on_device(): lax.ppermute(sent, ('mp', 'dp'), [(i, i ^ hop) for i in range(peers)])  9.99 us
  transfers between devices with their start and end apart: 13, of which 8 were waited for; matrix products, arithmetic and copies ran while one was open for 2% of the time, Pallas kernels for 0%

profile of v1, /device:TPU:0, one launch (start us, length us, event | category | flops | bytes accessed | tf_op | source)
XLA Modules:
  0.0 341.0 jit_solution(17475907546098905689)
XLA Ops:
  18.6 6.3 %all-to-all-start.1 = ((bf16[4,4,2048]{2,1,0:T(4,128)(2,1)}), bf16[4,4,2048]{2,1,0:T(4,128)(2,1)S(1)}, u32[]{:S(2)}, u32[]{:S(2)}) async-start(bf16[4,4,2048]{2,1,0:T(4,128)(2,1)} %reshape.292), calls=%async_computation.1 | async-start | bytes 131072 | tf_op jit(solution)/shard_map/all_to_all | solution.py:126
  26.4 4.3 %all-to-all-done.1 = bf16[4,4,2048]{2,1,0:T(4,128)(2,1)S(1)} async-done(((bf16[4,4,2048]{2,1,0:T(4,128)(2,1)}), bf16[4,4,2048]{2,1,0:T(4,128)(2,1)S(1)}, u32[]{:S(2)}, u32[]{:S(2)}) %all-to-all-start.1) | async-done | bytes 65568 | tf_op jit(solution)/shard_map/all_to_all | solution.py:126
  30.7 3.3 all-to-all-start
  34.7 5.0 %all-to-all-done = bf16[4,4,2048]{2,1,0:T(4,128)(2,1)S(1)} async-done(((bf16[4,4,2048]{2,1,0:T(4,128)(2,1)}), bf16[4,4,2048]{2,1,0:T(4,128)(2,1)S(1)}, u32[]{:S(2)}, u32[]{:S(2)}) %all-to-all-start) | async-done | bytes 65568 | tf_op jit(solution)/shard_map/all_to_all | solution.py:125
  40.4 24.4 %all_gather.13 = bf16[64,2048]{1,0:T(8,128)(2,1)S(1)} all-gather(bf16[8,2048]{1,0:T(8,128)(2,1)S(1)} %get-tuple-element.43), channel_id=1, replica_groups=mesh['section'=4,'mp'=2,'dp'=4] {'mp','dp'}, dimensions={0}, use_global_device_ids=true | all-gather | bytes 294912 | tf_op jit(solution)/shard_map/all_gather | solution.py:139
  64.9 24.3 %all_gather.12 = bf16[64,2048]{1,0:T(8,128)(2,1)S(1)} all-gather(bf16[8,2048]{1,0:T(8,128)(2,1)S(1)} %get-tuple-element.44), channel_id=1, replica_groups=mesh['section'=4,'mp'=2,'dp'=4] {'mp','dp'}, dimensions={0}, use_global_device_ids=true | all-gather | bytes 294912 | tf_op jit(solution)/shard_map/all_gather | solution.py:138
  89.1 3.0 fusion.40
  94.0 43.4 %all-reduce.6.cloned.1.call-done = f32[8,8,1024]{2,1,0:T(8,128)} async-done(((f32[8,8,1024]{2,1,0:T(8,128)}), f32[8,8,1024]{2,1,0:T(8,128)}) %all-reduce.6.cloned.1.call-update) | async-done | bytes 262160 | tf_op jit(solution)/shard_map/psum | solution.py:156
  145.8 3.4 collective-permute-done.1
  151.9 3.1 collective-permute-done.2
  155.7 8.9 %all-reduce.1 = (f32[8]{0:T(128)S(1)}, f32[64]{0:T(128)S(1)}) all-reduce(f32[8]{0:T(128)S(1)} %multiply_reduce_fusion.2, f32[64]{0:T(128)S(1)} %fusion.1), channel_id=1, replica_groups=mesh['section'=4,'mp'=2,'dp'=4] {'section'}, use_global_device_ids=true, to_apply=%region_4.7 | all-reduce | flops 72 | bytes 576 | tf_op jit(solution)/shard_map/psum | solution.py:166
  164.8 24.6 %all_gather.14 = bf16[64,2048]{1,0:T(8,128)(2,1)S(1)} all-gather(bf16[8,2048]{1,0:T(8,128)(2,1)S(1)} %multiply_convert_fusion), channel_id=1, replica_groups=mesh['section'=4,'mp'=2,'dp'=4] {'mp','dp'}, dimensions={0}, use_global_device_ids=true | all-gather | bytes 294912 | tf_op jit(solution)/shard_map/all_gather | solution.py:170
  189.4 4.3 %fusion.41 = f32[64,1024]{1,0:T(8,128)} fusion(bf16[64,2048]{1,0:T(8,128)(2,1)S(1)} %all_gather.14, bf16[1024,2048]{1,0:T(8,128)(2,1)} %param.21), kind=kOutput, calls=%fused_computation.130 | convolution fusion | flops 268435456 | bytes 4718592 | tf_op jit(solution)/shard_map/dot_general | solution.py:25
  195.9 5.1 %fusion.32 = s32[64]{0:T(128)S(1)} fusion(s32[64]{0:T(128)S(1)} %convert_reduce_fusion, s32[]{:T(128)} %bitcast.34, s32[]{:T(128)} %bitcast.30, s32[]{:T(128)} %bitcast.35, s32[]{:T(128)} %bitcast.31, s32[]{:T(128)} %bitcast.37, s32[]{:T(128)} %bitcast.36, s32[]{:T(128)} %bitcast.33, s32[]{:T(128)} %bitcast.32), kind=kLoop, calls=%fused_computation.113 | loop fusion | flops 2176 | bytes 544 | tf_op jit(solution)/shard_map/select_n | solution.py:145
  201.7 38.9 %all-reduce.8.cloned.1.call-done = (f32[64,1024]{1,0:T(8,128)}, f32[64,1024]{1,0:T(8,128)}) async-done(((f32[64,1024]{1,0:T(8,128)}, f32[64,1024]{1,0:T(8,128)}), (f32[64,1024]{1,0:T(8,128)}, f32[64,1024]{1,0:T(8,128)})) %all-reduce.8.cloned.1.call-update) | async-done | bytes 524304 | tf_op jit(solution)/shard_map/psum | solution.py:171
  241.8 15.9 %all-reduce = (f32[64]{0:T(128)S(1)}, f32[64]{0:T(128)S(1)}, f32[64]{0:T(128)S(1)}, f32[64]{0:T(128)S(1)}) all-reduce(f32[64]{0:T(128)S(1)} %get-tuple-element.6, f32[64]{0:T(128)S(1)} %get-tuple-element.8, f32[64]{0:T(128)S(1)} %get-tuple-element.7, f32[64]{0:T(128)S(1)} %get-tuple-element.5), channel_id=1, replica_groups=mesh['section'=4,'mp'=2,'dp'=4] {'mp','dp'}, use_global_device_ids=true, to_apply=%region_17.20 | all-reduce | flops 256 | bytes 2048 | tf_op jit(solution)/shard_map/psum | solution.py:173
  258.4 4.1 %fusion.8 = f32[64,2048]{1,0:T(8,128)} fusion(bf16[1024,2048]{1,0:T(8,128)(2,1)} %param.21, f32[64,1024]{1,0:T(8,128)} %get-tuple-element.16, f32[64,1024]{1,0:T(8,128)} %get-tuple-element.15, f32[64]{0:T(128)S(1)} %get-tuple-element.31, f32[64]{0:T(128)S(1)} %get-tuple-element.32, f32[64]{0:T(128)S(1)} %get-tuple-element.29, s32[64]{0:T(128)S(1)} %broadcast_subtract_fusion), kind=kOutput, calls=%fused_computation.23 | convolution fusion | flops 269025280 | bytes 5243904 | tf_op jit(solution)/shard_map/dot_general | solution.py:177
  262.5 31.1 %reduce-scatter.2.cloned.1.call-done = f32[8,2048]{1,0:T(8,128)} async-done(((f32[64,2048]{1,0:T(8,128)}), f32[8,2048]{1,0:T(8,128)}) %reduce-scatter.2.cloned.1.call-update) | async-done | bytes 65552 | tf_op jit(solution)/shard_map/reduce_scatter | solution.py:176
  294.6 9.9 %psum.79 = f32[8]{0:T(128)S(1)} all-reduce(f32[8]{0:T(128)S(1)} %multiply_reduce_fusion.1), channel_id=1, replica_groups=mesh['section'=4,'mp'=2,'dp'=4] {'section'}, use_global_device_ids=true, to_apply=%region_21.24 | all-reduce | flops 8 | bytes 64 | tf_op jit(solution)/shard_map/psum | solution.py:183
  305.4 8.3 %all_gather.15 = bf16[8,8192]{1,0:T(8,128)(2,1)} all-gather(bf16[8,2048]{1,0:T(8,128)(2,1)S(1)} %subtract_convert_fusion.2), channel_id=1, replica_groups=mesh['section'=4,'mp'=2,'dp'=4] {'section'}, dimensions={1}, use_global_device_ids=true | all-gather | bytes 163840 | tf_op jit(solution)/shard_map/all_gather | solution.py:187
  313.7 3.4 all-to-all-start.2
  317.8 6.2 %all-to-all-done.2 = bf16[8,8,1024]{2,0,1:T(8,128)(2,1)S(1)} async-done(((bf16[8,8,1024]{2,0,1:T(8,128)(2,1)}), bf16[8,8,1024]{2,0,1:T(8,128)(2,1)S(1)}, u32[]{:S(2)}, u32[]{:S(2)}) %all-to-all-start.2) | async-done | bytes 131104 | tf_op jit(solution)/shard_map/all_to_all | solution.py:188
  324.0 4.7 %fusion.9 = f32[2048,1024]{1,0:T(8,128)} fusion(bf16[64,2048]{1,0:T(8,128)(2,1)S(1)} %all_gather.13, bf16[8,8,1024]{2,0,1:T(8,128)(2,1)S(1)} %all-to-all-done.2), kind=kOutput, calls=%fused_computation.24 | convolution fusion | flops 268435456 | bytes 8781824 | tf_op jit(solution)/shard_map/dot_general | solution.py:31
  328.7 4.7 %fusion.11 = f32[2048,1024]{1,0:T(8,128)} fusion(bf16[64,2048]{1,0:T(8,128)(2,1)S(1)} %all_gather.12, bf16[8,8,1024]{2,0,1:T(8,128)(2,1)S(1)} %all-to-all-done.2), kind=kOutput, calls=%fused_computation.26 | convolution fusion | flops 268435456 | bytes 8781824 | tf_op jit(solution)/shard_map/dot_general | solution.py:31
  (89 shorter events, 33.2 us)
Async XLA Ops:
  7.2 8.1 %copy-start = (bf16[1,256,2048]{2,1,0:T(8,128)(2,1)S(1)}, bf16[1,256,2048]{2,1,0:T(8,128)(2,1)}, u32[]{:S(2)}) copy-start(bf16[1,256,2048]{2,1,0:T(8,128)(2,1)} %param.14) | copy-start | bytes 3145732
  18.6 12.1 %all-to-all-start.1 = ((bf16[4,4,2048]{2,1,0:T(4,128)(2,1)}), bf16[4,4,2048]{2,1,0:T(4,128)(2,1)S(1)}, u32[]{:S(2)}, u32[]{:S(2)}) async-start(bf16[4,4,2048]{2,1,0:T(4,128)(2,1)} %reshape.292), calls=%async_computation.1 | async-start | bytes 131072 | tf_op jit(solution)/shard_map/all_to_all | solution.py:126
  30.7 9.0 %all-to-all-start = ((bf16[4,4,2048]{2,1,0:T(4,128)(2,1)}), bf16[4,4,2048]{2,1,0:T(4,128)(2,1)S(1)}, u32[]{:S(2)}, u32[]{:S(2)}) async-start(bf16[4,4,2048]{2,1,0:T(4,128)(2,1)} %reshape.290), calls=%async_computation | async-start | bytes 131072 | tf_op jit(solution)/shard_map/all_to_all | solution.py:125
  34.0 103.4 %all-reduce.6.cloned.1.call-start = ((), (), s32[]{:S(2)}) async-start(), calls=%async_computation.4 | async-start | bytes 524288 | tf_op jit(solution)/shard_map/psum | solution.py:156
  40.3 51.8 %copy-start.2 = (bf16[2048,1024]{1,0:T(8,128)(2,1)S(1)}, bf16[2048,1024]{1,0:T(8,128)(2,1)}, u32[]{:S(2)}) copy-start(bf16[2048,1024]{1,0:T(8,128)(2,1)} %param.23) | copy-start | bytes 12582916
  92.2 63.5 %copy-start.5 = (s32[4,256]{1,0:T(4,128)S(1)}, s32[4,256]{1,0:T(4,128)}, u32[]{:S(2)}) copy-start(s32[4,256]{1,0:T(4,128)} %param.16) | copy-start | bytes 12292
  92.2 72.5 %copy-start.3 = (f32[2048]{0:T(1024)S(1)}, f32[2048]{0:T(1024)}, u32[]{:S(2)}) copy-start(f32[2048]{0:T(1024)} %param.20) | copy-start | bytes 24580
  93.7 99.9 %copy-start.4 = (f32[2048]{0:T(1024)S(1)}, f32[2048]{0:T(1024)}, u32[]{:S(2)}) copy-start(f32[2048]{0:T(1024)} %param.19) | copy-start | bytes 24580
  93.8 146.8 %all-reduce.8.cloned.1.call-start = ((), (), s32[]{:S(2)}) async-start(), calls=%async_computation.6 | async-start | bytes 1048576 | tf_op jit(solution)/shard_map/psum | solution.py:171
  138.3 6.0 %collective-permute-start = (f32[8,1024]{1,0:T(8,128)S(1)}, f32[8,1024]{1,0:T(8,128)S(1)}, u32[]{:S(2)}, u32[]{:S(2)}) collective-permute-start(f32[8,1024]{1,0:T(8,128)S(1)} %get-tuple-element.25), channel_id=1, source_target_pairs={{0,1},{1,0},{2,3},{3,2},{4,5},{5,4},{6,7},{7,6},{8,9},{9,8},{10,11... | collective-permute-start | bytes 98312 | tf_op jit(solution)/shard_map/ppermute | solution.py:162
  140.0 15.0 %collective-permute-start.6 = (f32[8,1024]{1,0:T(8,128)S(1)}, f32[8,1024]{1,0:T(8,128)S(1)}, u32[]{:S(2)}, u32[]{:S(2)}) collective-permute-start(f32[8,1024]{1,0:T(8,128)S(1)} %get-tuple-element.19), channel_id=1, source_target_pairs={{0,7},{1,6},{2,5},{3,4},{4,3},{5,2},{6,1},{7,0},{8,15},{9,14},{10,... | collective-permute-start | bytes 98312 | tf_op jit(solution)/shard_map/ppermute | solution.py:162
  141.2 13.8 %collective-permute-start.5 = (f32[8,1024]{1,0:T(8,128)S(1)}, f32[8,1024]{1,0:T(8,128)S(1)}, u32[]{:S(2)}, u32[]{:S(2)}) collective-permute-start(f32[8,1024]{1,0:T(8,128)S(1)} %get-tuple-element.20), channel_id=1, source_target_pairs={{0,6},{1,7},{2,4},{3,5},{4,2},{5,3},{6,0},{7,1},{8,14},{9,15},{10,... | collective-permute-start | bytes 98312 | tf_op jit(solution)/shard_map/ppermute | solution.py:162
  141.8 13.1 %collective-permute-start.4 = (f32[8,1024]{1,0:T(8,128)S(1)}, f32[8,1024]{1,0:T(8,128)S(1)}, u32[]{:S(2)}, u32[]{:S(2)}) collective-permute-start(f32[8,1024]{1,0:T(8,128)S(1)} %get-tuple-element.21), channel_id=1, source_target_pairs={{0,5},{1,4},{2,7},{3,6},{4,1},{5,0},{6,3},{7,2},{8,13},{9,12},{10,... | collective-permute-start | bytes 98312 | tf_op jit(solution)/shard_map/ppermute | solution.py:162
  142.9 12.1 %collective-permute-start.3 = (f32[8,1024]{1,0:T(8,128)S(1)}, f32[8,1024]{1,0:T(8,128)S(1)}, u32[]{:S(2)}, u32[]{:S(2)}) collective-permute-start(f32[8,1024]{1,0:T(8,128)S(1)} %get-tuple-element.22), channel_id=1, source_target_pairs={{0,4},{1,5},{2,6},{3,7},{4,0},{5,1},{6,2},{7,3},{8,12},{9,13},{10,... | collective-permute-start | bytes 98312 | tf_op jit(solution)/shard_map/ppermute | solution.py:162
  144.3 4.9 %collective-permute-start.1 = (f32[8,1024]{1,0:T(8,128)S(1)}, f32[8,1024]{1,0:T(8,128)S(1)}, u32[]{:S(2)}, u32[]{:S(2)}) collective-permute-start(f32[8,1024]{1,0:T(8,128)S(1)} %get-tuple-element.24), channel_id=1, source_target_pairs={{0,2},{1,3},{2,0},{3,1},{4,6},{5,7},{6,4},{7,5},{8,10},{9,11},{10,... | collective-permute-start | bytes 98312 | tf_op jit(solution)/shard_map/ppermute | solution.py:162
  149.2 5.7 %collective-permute-start.2 = (f32[8,1024]{1,0:T(8,128)S(1)}, f32[8,1024]{1,0:T(8,128)S(1)}, u32[]{:S(2)}, u32[]{:S(2)}) collective-permute-start(f32[8,1024]{1,0:T(8,128)S(1)} %get-tuple-element.23), channel_id=1, source_target_pairs={{0,3},{1,2},{2,1},{3,0},{4,7},{5,6},{6,5},{7,4},{8,11},{9,10},{10,... | collective-permute-start | bytes 98312 | tf_op jit(solution)/shard_map/ppermute | solution.py:162
  164.7 29.0 %copy-start.1 = (bf16[1024,2048]{1,0:T(8,128)(2,1)S(1)}, bf16[1024,2048]{1,0:T(8,128)(2,1)}, u32[]{:S(2)}) copy-start(bf16[1024,2048]{1,0:T(8,128)(2,1)} %param.21) | copy-start | bytes 12582916
  195.8 97.8 %reduce-scatter.2.cloned.1.call-start = ((), (), s32[]{:S(2)}) async-start(), calls=%async_computation.5 | async-start | bytes 589824 | tf_op jit(solution)/shard_map/reduce_scatter | solution.py:176
  313.7 10.2 %all-to-all-start.2 = ((bf16[8,8,1024]{2,0,1:T(8,128)(2,1)}), bf16[8,8,1024]{2,0,1:T(8,128)(2,1)S(1)}, u32[]{:S(2)}, u32[]{:S(2)}) async-start(bf16[8,8,1024]{2,0,1:T(8,128)(2,1)} %bitcast.39), calls=%async_computation.3 | async-start | bytes 262144 | tf_op jit(solution)/shard_map/all_to_all | solution.py:188
Sparse Core Ops, SparseCore 0:
  93.9 43.4 all-reduce.5
  195.9 44.5 all-reduce.7
  262.6 30.9 reduce-scatter.1
